TPU v7x, 256 devices: a whole 4x4x8 slice. The times are simulated.
256 devices in a mesh: circ: 8 (over y_lo, x), span: 32 (over y_hi, z, core).
Axes of the slice: x: 4, y: 4 (y_hi: 2, y_lo: 2; y = y_hi * 2 + y_lo), z: 8, core: 2. Of those that a mesh axis runs over, the one named last changes fastest.
Arguments:
- q_old: float32 [5, 32, 4096, 128], P(None, 'circ', 'span'), may hold values from -6 to 6
- pseudo_rate: float32 [32, 4096, 128], P('circ', 'span'), may hold values from 0.15 to 0.45
- flux_jacobians: float32 [3, 5, 5], replicated, may hold values from -2.5 to 2.5
- rotor_face: float32 [5, 32, 4096], P(None, 'circ', 'span'), may hold values from -6 to 6
- offsets: int32 [4096], P('span'), may hold values from 0 to 31
- owners: int32 [8, 128, 4], P('circ', 'span'), may hold values from 0 to 31, all different within a row; in each aligned block of 4 rows (0 to 3, 4 to 7, ..., all dimensions but the last counted through in order) at most 2 rows name the same one
- slots: int32 [8, 128, 4], P('circ', 'span'), may hold values from 0 to 3
- weight_idx: int32 [8, 128, 4], P('circ', 'span'), may hold values from 0 to 15
- weight_table: float32 [16], replicated, may hold values from 0.3 to 1
Outputs:
- q_new: float32 [5, 32, 4096, 128], P(None, 'circ', 'span')
Inputs may be any that keep to these rules, and one draw needn't show every extreme that they name: The 4 owners of one rotor panel differ; among the 4 rotor panels of one device in one circumferential block, no owner is named more than 2 times, and that count is reached.
All inputs are finite; a program needn't handle non-finite values.
Results may differ from a plain program's by a relative error of at most 0.000068.
Values sent between devices are 32-bit elements; how exact they have to be, the bound alone decides.
No kernel may reach another device: no remote copies, remote signals or barrier semaphores. Data moves between devices by JAX's collectives and lax.ppermute only.
A program may use at most 64 MiB of HBM per device.

v0:
```python
import jax
import jax.numpy as jnp
from jax import lax
from jax.sharding import PartitionSpec as P

NF = 5
KP_DEV = 4
PW = 32
inv_step = 0.5
viscosity = 0.1


def with_halo(block, sides, width):
    for axis, dim in sides:
        count = lax.axis_size(axis)
        forward = [(i, i + 1) for i in range(count - 1)]
        forward.append((count - 1, 0))
        backward = [(target, source) for source, target in forward]
        low = lax.ppermute(
            lax.slice_in_dim(block, block.shape[dim] - width, None, axis=dim), axis, forward
        )
        high = lax.ppermute(lax.slice_in_dim(block, 0, width, axis=dim), axis, backward)
        block = jnp.concatenate([low, block, high], axis=dim)
    return block


def contract(matrix, values):
    return jnp.einsum("fg,gtsa->ftsa", matrix, values, precision=lax.Precision.HIGHEST)


def advance(padded, current, previous, rate_cells, inlet_plane, jacobians):
    circ_up = padded[:, 2:, 1:-1]
    circ_down = padded[:, :-2, 1:-1]
    span_up = padded[:, 1:-1, 2:]
    span_down = padded[:, 1:-1, :-2]
    zero_column = jnp.zeros_like(current[..., :1])
    axial_up = jnp.concatenate([current[..., 1:], zero_column], axis=-1)
    axial_down = jnp.concatenate([inlet_plane[..., None], current[..., :-1]], axis=-1)
    convection = contract(jacobians[0], circ_up - circ_down)
    convection = convection + contract(jacobians[1], span_up - span_down)
    convection = convection + contract(jacobians[2], axial_up - axial_down)
    laplacian = (
        circ_up + circ_down + (span_up + span_down) + (axial_up + axial_down) - 6.0 * current
    )
    residual = inv_step * (current - previous) + 0.5 * convection - viscosity * laplacian
    return current - rate_cells[None] * residual


def wall_zero(field_array, width):
    span_index = lax.axis_index("span")
    span_count = lax.axis_size("span")
    length = field_array.shape[2]
    position = jnp.arange(length, dtype=jnp.int32)
    at_hub = jnp.logical_and(span_index == 0, position < width)
    at_tip = jnp.logical_and(span_index == span_count - 1, position >= length - width)
    keeping = jnp.logical_not(jnp.logical_or(at_hub, at_tip)).astype(field_array.dtype)
    keeping = keeping.reshape(1, 1, length, 1)
    return field_array * keeping


def body(
    q_old, pseudo_rate, flux_jacobians, rotor_face, offsets, owners, slots, weight_idx, weight_table
):
    circ_count = lax.axis_size("circ")
    rows_local = rotor_face.shape[1]
    total_rows = rows_local * circ_count
    row_iota = jnp.arange(rows_local, dtype=jnp.int32)
    all_rows = lax.all_gather(rotor_face, "circ", axis=1, tiled=True)
    first_row = lax.axis_index("circ") * rows_local
    source_rows = (first_row + row_iota[:, None] - offsets[None, :]) % total_rows
    rotated = jnp.take_along_axis(all_rows, source_rows[None], axis=1)
    panels = rotated.reshape(NF, rows_local, KP_DEV, PW)
    table_ids = jnp.arange(weight_table.shape[0], dtype=jnp.int32)
    weights = jnp.sum(jnp.where(weight_idx[..., None] == table_ids, weight_table, 0.0), axis=-1)
    targets = owners[0] * KP_DEV + slots[0]
    local_weights = weights[0]
    panel_ids = jnp.arange(KP_DEV * lax.axis_size("span"), dtype=jnp.int32)
    mixing = jnp.sum(
        jnp.where(targets[None] == panel_ids[:, None, None], local_weights[None], 0.0), axis=-1
    )
    own_panels = lax.psum_scatter(
        jnp.einsum("gk,ftkp->gftp", mixing, panels, precision=lax.Precision.HIGHEST),
        "span",
        scatter_dimension=0,
        tiled=True,
    )
    inlet_plane = jnp.transpose(own_panels, (1, 2, 0, 3)).reshape(NF, rows_local, KP_DEV * PW)

    def sweep(current):
        padded = with_halo(current, (("circ", 1), ("span", 2)), 1)
        padded = wall_zero(padded, 1)
        return advance(padded, current, q_old, pseudo_rate, inlet_plane, flux_jacobians)

    first_pass = sweep(q_old)
    return sweep(first_pass)


def solution(mesh):
    return jax.shard_map(
        body,
        mesh=mesh,
        in_specs=(
            P(None, "circ", "span", None),
            P("circ", "span", None),
            P(),
            P(None, "circ", "span"),
            P("span"),
            P("circ", "span", None),
            P("circ", "span", None),
            P("circ", "span", None),
            P(),
        ),
        out_specs=P(None, "circ", "span", None),
        check_vma=False,
    )
```

profile of v0, /device:TPU:6, one launch (start us, length us, event | category | flops | bytes accessed | tf_op | source)
XLA Modules:
  0.0 389.9 jit_solution(16798565273600464727)
XLA Ops:
  6.5 1.1 fusion.53
  8.7 1.6 collective-permute-start
  12.1 37.0 %all_gather.3 = f32[5,32,128]{2,0,1:T(8,128)S(1)} all-gather(f32[5,4,128]{2,0,1:T(8,128)S(1)} %copy.72), channel_id=1, replica_groups=mesh['circ'=8,'span'=32] {'circ'}, dimensions={1}, use_global_device_ids=true | all-gather | bytes 92160 | tf_op jit(solution)/shard_map/all_gather | solution.py:68
  49.8 5.9 %gather_fusion = f32[512,5]{1,0:T(8,128)} fusion(f32[5,32,128]{0,2,1:T(8,128)S(1)} %copy.73, s32[512]{0:T(512)S(1)} %fusion.43), kind=kCustom, calls=%fused_computation | custom fusion | bytes 24576 | tf_op jit(solution)/shard_map/jit(take_along_axis)/gather | solution.py:71
  55.7 1.1 copy.87
  57.1 2.3 fusion.34
  59.5 1.5 fusion.54
  61.0 3.4 copy.106
  64.4 2.1 copy.105
  67.9 264.7 %all-reduce.5.cloned.1.call-done = f32[128,5,4,32]{3,0,2,1:T(8,128)} async-done(((f32[128,5,4,32]{3,0,2,1:T(8,128)}), f32[128,5,4,32]{3,0,2,1:T(8,128)}) %all-reduce.5.cloned.1.call-update) | async-done | bytes 327696
  334.3 1.1 constant_dynamic-update-slice_fusion.1
  336.2 1.5 constant_dynamic-update-slice_fusion
  338.0 5.8 %collective-permute-start.3 = (f32[5,6,1,128]{3,0,2,1:T(8,128)S(1)}, f32[5,6,1,128]{3,0,2,1:T(8,128)S(1)}, u32[]{:S(2)}, u32[]{:S(2)}) collective-permute-start(f32[5,6,1,128]{3,0,2,1:T(8,128)S(1)} %get-tuple-element.8), channel_id=1, source_target_pairs={{1,0},{2,1},{3,2},{4,3},{5,4},{6,5},{7,6},{8,7},{9,8},{10,9},{11,1... | collective-permute-start | bytes 46088 | tf_op jit(solution)/shard_map/ppermute | solution.py:22
  343.8 2.5 fusion.18
  346.6 2.0 fusion.20
  348.7 4.9 %fusion.7 = f32[5,4,128,128]{3,0,2,1:T(8,128)S(1)} fusion(f32[4,128,128,5]{2,3,1,0:T(8,128)S(1)} %fusion.18, f32[4,128,128,5]{2,3,1,0:T(8,128)S(1)} %fusion.20, f32[5,6,130,128]{3,0,2,1:T(8,128)S(1)} %maximum_multiply_fusion, f32[5,4,128,127]{3,0,2,1:T(8,128)S(1)} %copy-done.2, f32[4,128,128]{2,1,0:T(8,128)S(1)} %copy-done.3, ...), kind=kOutput, calls=%fused_computation.14 | convolution fusion | flops 25559040 | bytes 25954816 | tf_op jit(solution)/shard_map/fg,gtsa->ftsa/dot_general | solution.py:28
  354.3 1.5 collective-permute-start.5
  356.5 6.5 %collective-permute-done.4 = f32[5,1,128,128]{3,0,2,1:T(8,128)S(1)} collective-permute-done((f32[5,1,128,128]{3,0,2,1:T(8,128)S(1)}, f32[5,1,128,128]{3,0,2,1:T(8,128)S(1)}, u32[]{:S(2)}, u32[]{:S(2)}) %collective-permute-start.4) | collective-permute-done | bytes 327712 | tf_op jit(solution)/shard_map/ppermute | solution.py:19
  362.9 2.7 collective-permute-done.5
  365.7 6.1 %collective-permute-start.7 = (f32[5,6,1,128]{3,0,2,1:T(8,128)S(1)}, f32[5,6,1,128]{3,0,2,1:T(8,128)S(1)}, u32[]{:S(2)}, u32[]{:S(2)}) collective-permute-start(f32[5,6,1,128]{3,0,2,1:T(8,128)S(1)} %get-tuple-element.6), channel_id=1, source_target_pairs={{1,0},{2,1},{3,2},{4,3},{5,4},{6,5},{7,6},{8,7},{9,8},{10,9},{11,1... | collective-permute-start | bytes 46088 | tf_op jit(solution)/shard_map/ppermute | solution.py:22
  371.8 2.5 fusion.8
  374.7 2.0 fusion.10
  376.7 5.0 %fusion.3 = f32[5,4,128,128]{3,0,2,1:T(8,128)S(1)} fusion(f32[5,4,128,128]{3,0,2,1:T(8,128)S(1)} %fusion.7, f32[4,128,128,5]{2,3,1,0:T(8,128)S(1)} %fusion.8, f32[4,128,128,5]{2,3,1,0:T(8,128)S(1)} %fusion.10, f32[5,6,130,128]{3,0,2,1:T(8,128)S(1)} %maximum_multiply_fusion.1, f32[5,4,128,127]{3,0,2,1:T(8,128)S(1)} %get-tuple-element.12, ...), kind=kOutput, calls=%fused_computation.9 | convolution fusion | flops 25559040 | bytes 28051968 | tf_op jit(solution)/shard_map/fg,gtsa->ftsa/dot_general | solution.py:28
  381.7 1.3 copy.82
  (60 shorter events, 9.4 us)
Async XLA Ops:
  6.5 5.3 %copy-start.9 = (s32[128]{0:T(128)S(1)}, s32[128]{0:T(128)}, u32[]{:S(2)}) copy-start(s32[128]{0:T(128)} %param.13) | copy-start | bytes 1540
  6.5 5.6 %copy-start.4 = (f32[5,4,128]{2,1,0:T(4,128)S(1)}, f32[5,4,128]{2,1,0:T(4,128)}, u32[]{:S(2)}) copy-start(f32[5,4,128]{2,1,0:T(4,128)} %param.12) | copy-start | bytes 30724
  6.5 326.1 %all-reduce.5.cloned.1.call-start = ((), (), s32[]{:S(2)}) async-start(), calls=%async_computation | async-start | bytes 2621440
  8.7 48.1 %copy-start.6 = (s32[1,4,4]{2,1,0:T(4,128)S(1)}, s32[1,4,4]{2,1,0:T(4,128)}, u32[]{:S(2)}) copy-start(s32[1,4,4]{2,1,0:T(4,128)} %param.15) | copy-start | bytes 196
  8.7 48.1 %copy-start.7 = (s32[1,4,4]{2,1,0:T(4,128)S(1)}, s32[1,4,4]{2,1,0:T(4,128)}, u32[]{:S(2)}) copy-start(s32[1,4,4]{2,1,0:T(4,128)} %param.14) | copy-start | bytes 196
  8.7 48.2 %copy-start.8 = (s32[1,4,4]{2,1,0:T(4,128)S(1)}, s32[1,4,4]{2,1,0:T(4,128)}, u32[]{:S(2)}) copy-start(s32[1,4,4]{2,1,0:T(4,128)} %param.16) | copy-start | bytes 196
  8.7 48.2 %copy-start.10 = (f32[16]{0:T(128)S(1)}, f32[16]{0:T(128)}, u32[]{:S(2)}) copy-start(f32[16]{0:T(128)} %param.17) | copy-start | bytes 196
  8.7 325.6 %collective-permute-start = (f32[5,1,128,128]{3,0,2,1:T(8,128)}, f32[5,1,128,128]{3,0,2,1:T(8,128)}, u32[]{:S(2)}, u32[]{:S(2)}) collective-permute-start(f32[5,1,128,128]{3,0,2,1:T(8,128)} %copy.107), channel_id=1, source_target_pairs={{0,32},{32,64},{64,96},{96,128},{128,160},{160,192},{192,224},{224... | collective-permute-start | bytes 983048 | tf_op jit(solution)/shard_map/ppermute | solution.py:19
  11.3 324.9 %collective-permute-start.1 = (f32[5,1,128,128]{3,0,2,1:T(8,128)}, f32[5,1,128,128]{3,0,2,1:T(8,128)}, u32[]{:S(2)}, u32[]{:S(2)}) collective-permute-start(f32[5,1,128,128]{3,0,2,1:T(8,128)} %copy.108), channel_id=1, source_target_pairs={{32,0},{64,32},{96,64},{128,96},{160,128},{192,160},{224,192},{0,2... | collective-permute-start | bytes 983048 | tf_op jit(solution)/shard_map/ppermute | solution.py:22
  49.8 9.7 %copy-start = (f32[5,4,128,128]{3,2,1,0:T(8,128)S(1)}, f32[5,4,128,128]{3,2,1,0:T(8,128)}, u32[]{:S(2)}) copy-start(f32[5,4,128,128]{3,2,1,0:T(8,128)} %param.9) | copy-start | bytes 3932164
  64.4 2.2 copy-start.11
  64.4 3.4 copy-start.5
  335.4 8.4 %copy-start.1 = (f32[5,4,128,127]{3,0,2,1:T(8,128)S(1)}, f32[5,4,128,127]{3,0,2,1:T(8,128)}, u32[]{:S(2)}) copy-start(f32[5,4,128,127]{3,0,2,1:T(8,128)} %copy.106) | copy-start | bytes 3901444
  335.4 8.4 %copy-start.2 = (f32[5,4,128,127]{3,0,2,1:T(8,128)S(1)}, f32[5,4,128,127]{3,0,2,1:T(8,128)}, u32[]{:S(2)}) copy-start(f32[5,4,128,127]{3,0,2,1:T(8,128)} %copy.105) | copy-start | bytes 3901444
  337.8 8.5 %collective-permute-start.2 = (f32[5,6,1,128]{3,0,2,1:T(8,128)S(1)}, f32[5,6,1,128]{3,0,2,1:T(8,128)S(1)}, u32[]{:S(2)}, u32[]{:S(2)}) collective-permute-start(f32[5,6,1,128]{3,0,2,1:T(8,128)S(1)} %get-tuple-element.7), channel_id=1, source_target_pairs={{0,1},{1,2},{2,3},{3,4},{4,5},{5,6},{6,7},{7,8},{8,9},{9,10},{10,1... | collective-permute-start | bytes 46088 | tf_op jit(solution)/shard_map/ppermute | solution.py:19
  338.0 8.3 %collective-permute-start.3 = (f32[5,6,1,128]{3,0,2,1:T(8,128)S(1)}, f32[5,6,1,128]{3,0,2,1:T(8,128)S(1)}, u32[]{:S(2)}, u32[]{:S(2)}) collective-permute-start(f32[5,6,1,128]{3,0,2,1:T(8,128)S(1)} %get-tuple-element.8), channel_id=1, source_target_pairs={{1,0},{2,1},{3,2},{4,3},{5,4},{6,5},{7,6},{8,7},{9,8},{10,9},{11,1... | collective-permute-start | bytes 46088 | tf_op jit(solution)/shard_map/ppermute | solution.py:22
  346.6 2.0 copy-start.3
  353.7 9.3 %collective-permute-start.4 = (f32[5,1,128,128]{3,0,2,1:T(8,128)S(1)}, f32[5,1,128,128]{3,0,2,1:T(8,128)S(1)}, u32[]{:S(2)}, u32[]{:S(2)}) collective-permute-start(f32[5,1,128,128]{3,0,2,1:T(8,128)S(1)} %get-tuple-element.9), channel_id=1, source_target_pairs={{0,32},{32,64},{64,96},{96,128},{128,160},{160,192},{192,224},{224... | collective-permute-start | bytes 983048 | tf_op jit(solution)/shard_map/ppermute | solution.py:19
  354.3 11.3 %collective-permute-start.5 = (f32[5,1,128,128]{3,0,2,1:T(8,128)S(1)}, f32[5,1,128,128]{3,0,2,1:T(8,128)S(1)}, u32[]{:S(2)}, u32[]{:S(2)}) collective-permute-start(f32[5,1,128,128]{3,0,2,1:T(8,128)S(1)} %get-tuple-element.10), channel_id=1, source_target_pairs={{32,0},{64,32},{96,64},{128,96},{160,128},{192,160},{224,192},{0,2... | collective-permute-start | bytes 983048 | tf_op jit(solution)/shard_map/ppermute | solution.py:22
  365.6 8.7 %collective-permute-start.6 = (f32[5,6,1,128]{3,0,2,1:T(8,128)S(1)}, f32[5,6,1,128]{3,0,2,1:T(8,128)S(1)}, u32[]{:S(2)}, u32[]{:S(2)}) collective-permute-start(f32[5,6,1,128]{3,0,2,1:T(8,128)S(1)} %get-tuple-element.5), channel_id=1, source_target_pairs={{0,1},{1,2},{2,3},{3,4},{4,5},{5,6},{6,7},{7,8},{8,9},{9,10},{10,1... | collective-permute-start | bytes 46088 | tf_op jit(solution)/shard_map/ppermute | solution.py:19
  365.7 8.6 %collective-permute-start.7 = (f32[5,6,1,128]{3,0,2,1:T(8,128)S(1)}, f32[5,6,1,128]{3,0,2,1:T(8,128)S(1)}, u32[]{:S(2)}, u32[]{:S(2)}) collective-permute-start(f32[5,6,1,128]{3,0,2,1:T(8,128)S(1)} %get-tuple-element.6), channel_id=1, source_target_pairs={{1,0},{2,1},{3,2},{4,3},{5,4},{6,5},{7,6},{8,7},{9,8},{10,9},{11,1... | collective-permute-start | bytes 46088 | tf_op jit(solution)/shard_map/ppermute | solution.py:22
Sparse Core Ops, SparseCore 0:
  59.6 272.9 all-reduce.4
where the time goes:
time: 390 us
  waiting for transfers between devices  274 us (70%)
  blocking collectives  37 us (9%)
  local copies, waits for them, and re-layouts  25.8 us (7%)
  matrix products  21.3 us (5%)
  starting transfers between devices  16.4 us (4%)
  between operations  14.4 us (4%)
    unnamed x2, waiting for transfers between devices  265 us
    all_gather x1, blocking collectives, body(): all_rows = lax.all_gather(rotor_face, 'circ', axis=1, tiled=True)  37 us
    dot_general x6, matrix products, contract(): jnp.einsum('fg,gtsa->ftsa', matrix, values, precision=lax.Precision.HIGHEST)  18.9 us
    ppermute x4, starting transfers between devices, with_halo(): lax.ppermute(lax.slice_in_dim(block, 0, width, axis=dim), axis, backward)  13.8 us
    unnamed x32, local copies, waits for them, and re-layouts  10.2 us
  transfers between devices with their start and end apart: 9, of which 3 were waited for; matrix products, arithmetic and copies ran while one was open for 7% of the time, Pallas kernels for 0%

commit v1 on v0

--- a/solution.py
+++ b/solution.py
@@ -65,7 +65,9 @@
     rows_local = rotor_face.shape[1]
     total_rows = rows_local * circ_count
     row_iota = jnp.arange(rows_local, dtype=jnp.int32)
-    all_rows = lax.all_gather(rotor_face, "circ", axis=1, tiled=True)
+    all_rows = jnp.concatenate(
+        lax.all_to_all(jnp.stack([rotor_face] * lax.axis_size("circ")), "circ", 0, 0), axis=1
+    )
     first_row = lax.axis_index("circ") * rows_local
     source_rows = (first_row + row_iota[:, None] - offsets[None, :]) % total_rows
     rotated = jnp.take_along_axis(all_rows, source_rows[None], axis=1)

time: 390 us -> 373 us (0.956)
  blocking collectives: 37 us -> 0 us
  matrix products: 21.3 us -> 27.2 us
  starting transfers between devices: 16.4 us -> 22.1 us
  local copies, waits for them, and re-layouts: 25.8 us -> 30.1 us
    all_gather x1 -> x0, blocking collectives: 37 us -> none  [body(): all_rows = lax.all_gather(rotor_face, 'circ', axis=1, tiled=True)]
    dot_general x6, matrix products: 18.9 us -> 24.9 us  [contract(): jnp.einsum('fg,gtsa->ftsa', matrix, values, precision=lax.Precision.HIGHEST)]
    all_to_all x0 -> x1, starting transfers between devices: none -> 5.79 us  [body(): lax.all_to_all(jnp.stack([rotor_face] * lax.axis_size('circ')), 'circ', 0...]
    ppermute x4, waiting for transfers between devices: 6.49 us -> 11.3 us  [with_halo(): lax.ppermute(lax.slice_in_dim(block, block.shape[dim] - width, None, axis...]
    unnamed x32 -> x35, local copies, waits for them, and re-layouts: 10.2 us -> 13.5 us
  transfers between devices with their start and end apart: 9 -> 10, of which waited for: 3 -> 3; matrix products, arithmetic and copies ran while one was open for 7% -> 9% of each run, Pallas kernels for 0% -> 0%
where the time goes in v1:
time: 373 us
  waiting for transfers between devices  276 us (74%)
  local copies, waits for them, and re-layouts  30.1 us (8%)
  matrix products  27.2 us (7%)
  starting transfers between devices  22.1 us (6%)
  between operations  14.4 us (4%)
    unnamed x2, waiting for transfers between devices  262 us
    dot_general x6, matrix products, contract(): jnp.einsum('fg,gtsa->ftsa', matrix, values, precision=lax.Precision.HIGHEST)  24.9 us
    ppermute x4, starting transfers between devices, with_halo(): lax.ppermute(lax.slice_in_dim(block, 0, width, axis=dim), axis, backward)  13.8 us
    unnamed x35, local copies, waits for them, and re-layouts  13.5 us
    ppermute x4, waiting for transfers between devices, with_halo(): lax.ppermute(lax.slice_in_dim(block, block.shape[dim] - width, None, axis...  11.3 us
  transfers between devices with their start and end apart: 10, of which 3 were waited for; matrix products, arithmetic and copies ran while one was open for 9% of the time, Pallas kernels for 0%

profile of v1, /device:TPU:6, one launch (start us, length us, event | category | flops | bytes accessed | tf_op | source)
XLA Modules:
  0.0 372.8 jit_solution(6200574052720003767)
XLA Ops:
  6.5 1.5 stack.2
  8.0 5.8 %all-to-all-start = ((f32[8,5,4,128]{3,2,1,0:T(4,128)}), f32[8,5,4,128]{3,2,1,0:T(4,128)S(1)}, u32[]{:S(2)}, u32[]{:S(2)}) async-start(f32[8,5,4,128]{3,2,1,0:T(4,128)} %stack.2), calls=%async_computation | async-start | bytes 163840 | tf_op jit(solution)/shard_map/all_to_all | solution.py:69
  13.8 1.1 fusion.53
  15.9 1.5 collective-permute-start
  19.0 1.5 fusion.54
  20.6 3.5 copy.104
  24.1 2.2 copy.103
  28.6 5.9 %gather_fusion = f32[512,5]{1,0:T(8,128)} fusion(f32[5,32,128]{0,2,1:T(8,128)S(1)} %bitcast.64, s32[512]{0:T(512)S(1)} %fusion.43), kind=kCustom, calls=%fused_computation | custom fusion | bytes 24576 | tf_op jit(solution)/shard_map/jit(take_along_axis)/gather | solution.py:73
  38.7 1.6 copy-done.5
  40.3 6.8 %collective-permute-start.3 = (f32[5,6,1,128]{3,0,2,1:T(8,128)S(1)}, f32[5,6,1,128]{3,0,2,1:T(8,128)S(1)}, u32[]{:S(2)}, u32[]{:S(2)}) collective-permute-start(f32[5,6,1,128]{3,0,2,1:T(8,128)S(1)} %get-tuple-element.8), channel_id=1, source_target_pairs={{1,0},{2,1},{3,2},{4,3},{5,4},{6,5},{7,6},{8,7},{9,8},{10,9},{11,1... | collective-permute-start | bytes 46088 | tf_op jit(solution)/shard_map/ppermute | solution.py:22
  47.1 2.3 fusion.34
  49.4 2.2 maximum_multiply_fusion
  51.7 1.6 copy-done.3
  53.3 3.4 fusion.20
  56.7 262.3 %all-reduce.5.cloned.1.call-done = f32[128,5,4,32]{3,0,2,1:T(8,128)} async-done(((f32[128,5,4,32]{3,0,2,1:T(8,128)}), f32[128,5,4,32]{3,0,2,1:T(8,128)}) %all-reduce.5.cloned.1.call-update) | async-done | bytes 327696
  320.8 4.9 %fusion.18 = f32[4,128,128,5]{2,3,1,0:T(8,128)S(1)} fusion(f32[5,4,128,127]{3,0,2,1:T(8,128)} %copy.103, f32[5,4,128,127]{3,0,2,1:T(8,128)} %copy.104, f32[5,4,128,1]{3,0,2,1:T(8,128)S(1)} %copy.74, f32[1,5,5]{2,0,1:T(1,128)S(1)} %get-tuple-element.19), kind=kOutput, calls=%fused_computation.23 | convolution fusion | flops 20316160 | bytes 3922020 | tf_op jit(solution)/shard_map/fg,gtsa->ftsa/dot_general | solution.py:28
  325.7 7.1 %fusion.7 = f32[5,4,128,128]{3,0,2,1:T(8,128)S(1)} fusion(f32[4,128,128,5]{2,3,1,0:T(8,128)S(1)} %fusion.18, f32[4,128,128,5]{2,3,1,0:T(8,128)} %fusion.20, f32[5,6,130,128]{3,0,2,1:T(8,128)S(1)} %copy-done.4, f32[5,4,128,127]{3,0,2,1:T(8,128)S(1)} %copy-done.2, f32[4,128,128]{2,1,0:T(8,128)S(1)} %copy-done.6, f32[5,4,128,128]{3,2,1,0:T(8,128)S(1)} %copy-done, ...), kind=kOutput, calls=%fused_computation.14 | convolution fusion | flops 25559040 | bytes 25168384 | tf_op jit(solution)/shard_map/fg,gtsa->ftsa/dot_general | solution.py:28
  335.7 11.3 %collective-permute-done.4 = f32[5,1,128,128]{3,0,2,1:T(8,128)S(1)} collective-permute-done((f32[5,1,128,128]{3,0,2,1:T(8,128)S(1)}, f32[5,1,128,128]{3,0,2,1:T(8,128)S(1)}, u32[]{:S(2)}, u32[]{:S(2)}) %collective-permute-start.4) | collective-permute-done | bytes 327712 | tf_op jit(solution)/shard_map/ppermute | solution.py:19
  347.0 2.4 collective-permute-done.5
  349.4 5.3 %collective-permute-start.7 = (f32[5,6,1,128]{3,0,2,1:T(8,128)S(1)}, f32[5,6,1,128]{3,0,2,1:T(8,128)S(1)}, u32[]{:S(2)}, u32[]{:S(2)}) collective-permute-start(f32[5,6,1,128]{3,0,2,1:T(8,128)S(1)} %get-tuple-element.6), channel_id=1, source_target_pairs={{1,0},{2,1},{3,2},{4,3},{5,4},{6,5},{7,6},{8,7},{9,8},{10,9},{11,1... | collective-permute-start | bytes 46088 | tf_op jit(solution)/shard_map/ppermute | solution.py:22
  354.8 2.5 fusion.8
  357.7 2.0 fusion.10
  359.7 5.0 %fusion.3 = f32[5,4,128,128]{3,0,2,1:T(8,128)S(1)} fusion(f32[5,4,128,128]{3,0,2,1:T(8,128)S(1)} %fusion.7, f32[4,128,128,5]{2,3,1,0:T(8,128)S(1)} %fusion.8, f32[4,128,128,5]{2,3,1,0:T(8,128)S(1)} %fusion.10, f32[5,6,130,128]{3,0,2,1:T(8,128)S(1)} %maximum_multiply_fusion.1, f32[5,4,128,127]{3,0,2,1:T(8,128)S(1)} %get-tuple-element.12, ...), kind=kOutput, calls=%fused_computation.9 | convolution fusion | flops 25559040 | bytes 28051968 | tf_op jit(solution)/shard_map/fg,gtsa->ftsa/dot_general | solution.py:28
  364.7 1.3 copy.80
  (65 shorter events, 13.5 us)
Async XLA Ops:
  6.5 12.4 %copy-start = (f32[5,4,128,128]{3,2,1,0:T(8,128)S(1)}, f32[5,4,128,128]{3,2,1,0:T(8,128)}, u32[]{:S(2)}) copy-start(f32[5,4,128,128]{3,2,1,0:T(8,128)} %param.9) | copy-start | bytes 3932164
  8.0 20.0 %all-to-all-start = ((f32[8,5,4,128]{3,2,1,0:T(4,128)}), f32[8,5,4,128]{3,2,1,0:T(4,128)S(1)}, u32[]{:S(2)}, u32[]{:S(2)}) async-start(f32[8,5,4,128]{3,2,1,0:T(4,128)} %stack.2), calls=%async_computation | async-start | bytes 163840 | tf_op jit(solution)/shard_map/all_to_all | solution.py:69
  13.8 305.3 %all-reduce.5.cloned.1.call-start = ((), (), s32[]{:S(2)}) async-start(), calls=%async_computation.1 | async-start | bytes 2621440
  15.9 19.8 %collective-permute-start = (f32[5,1,128,128]{3,0,2,1:T(8,128)}, f32[5,1,128,128]{3,0,2,1:T(8,128)}, u32[]{:S(2)}, u32[]{:S(2)}) collective-permute-start(f32[5,1,128,128]{3,0,2,1:T(8,128)} %copy.105), channel_id=1, source_target_pairs={{0,32},{32,64},{64,96},{96,128},{128,160},{160,192},{192,224},{224... | collective-permute-start | bytes 983048 | tf_op jit(solution)/shard_map/ppermute | solution.py:19
  18.4 19.2 %collective-permute-start.1 = (f32[5,1,128,128]{3,0,2,1:T(8,128)}, f32[5,1,128,128]{3,0,2,1:T(8,128)}, u32[]{:S(2)}, u32[]{:S(2)}) collective-permute-start(f32[5,1,128,128]{3,0,2,1:T(8,128)} %copy.106), channel_id=1, source_target_pairs={{32,0},{64,32},{96,64},{128,96},{160,128},{192,160},{224,192},{0,2... | collective-permute-start | bytes 983048 | tf_op jit(solution)/shard_map/ppermute | solution.py:22
  19.0 1.5 copy-start.11
  19.0 1.6 copy-start.7
  24.0 2.2 copy-start.13
  24.0 3.4 copy-start.8
  24.0 3.4 copy-start.9
  24.0 3.5 copy-start.10
  24.0 3.5 copy-start.12
  38.7 1.6 copy-start.5
  40.3 9.1 %collective-permute-start.2 = (f32[5,6,1,128]{3,0,2,1:T(8,128)S(1)}, f32[5,6,1,128]{3,0,2,1:T(8,128)S(1)}, u32[]{:S(2)}, u32[]{:S(2)}) collective-permute-start(f32[5,6,1,128]{3,0,2,1:T(8,128)S(1)} %get-tuple-element.7), channel_id=1, source_target_pairs={{0,1},{1,2},{2,3},{3,4},{4,5},{5,6},{6,7},{7,8},{8,9},{9,10},{10,1... | collective-permute-start | bytes 46088 | tf_op jit(solution)/shard_map/ppermute | solution.py:19
  40.3 9.1 %collective-permute-start.3 = (f32[5,6,1,128]{3,0,2,1:T(8,128)S(1)}, f32[5,6,1,128]{3,0,2,1:T(8,128)S(1)}, u32[]{:S(2)}, u32[]{:S(2)}) collective-permute-start(f32[5,6,1,128]{3,0,2,1:T(8,128)S(1)} %get-tuple-element.8), channel_id=1, source_target_pairs={{1,0},{2,1},{3,2},{4,3},{5,4},{6,5},{7,6},{8,7},{9,8},{10,9},{11,1... | collective-permute-start | bytes 46088 | tf_op jit(solution)/shard_map/ppermute | solution.py:22
  51.7 1.7 copy-start.3
  320.7 4.9 %copy-start.1 = (f32[5,4,128,127]{3,0,2,1:T(8,128)S(1)}, f32[5,4,128,127]{3,0,2,1:T(8,128)}, u32[]{:S(2)}) copy-start(f32[5,4,128,127]{3,0,2,1:T(8,128)} %copy.104) | copy-start | bytes 3901444
  320.8 4.9 %copy-start.2 = (f32[5,4,128,127]{3,0,2,1:T(8,128)S(1)}, f32[5,4,128,127]{3,0,2,1:T(8,128)}, u32[]{:S(2)}) copy-start(f32[5,4,128,127]{3,0,2,1:T(8,128)} %copy.103) | copy-start | bytes 3901444
  320.8 4.9 %copy-start.4 = (f32[5,6,130,128]{3,0,2,1:T(8,128)S(1)}, f32[5,6,130,128]{3,0,2,1:T(8,128)}, u32[]{:S(2)}) copy-start(f32[5,6,130,128]{3,0,2,1:T(8,128)} %copy-done.3) | copy-start | bytes 5990404
  320.8 4.9 %copy-start.6 = (f32[4,128,128]{2,1,0:T(8,128)S(1)}, f32[4,128,128]{2,1,0:T(8,128)}, u32[]{:S(2)}) copy-start(f32[4,128,128]{2,1,0:T(8,128)} %param.10) | copy-start | bytes 786436
  332.9 14.1 %collective-permute-start.4 = (f32[5,1,128,128]{3,0,2,1:T(8,128)S(1)}, f32[5,1,128,128]{3,0,2,1:T(8,128)S(1)}, u32[]{:S(2)}, u32[]{:S(2)}) collective-permute-start(f32[5,1,128,128]{3,0,2,1:T(8,128)S(1)} %get-tuple-element.9), channel_id=1, source_target_pairs={{0,32},{32,64},{64,96},{96,128},{128,160},{160,192},{192,224},{224... | collective-permute-start | bytes 983048 | tf_op jit(solution)/shard_map/ppermute | solution.py:19
  333.9 15.5 %collective-permute-start.5 = (f32[5,1,128,128]{3,0,2,1:T(8,128)S(1)}, f32[5,1,128,128]{3,0,2,1:T(8,128)S(1)}, u32[]{:S(2)}, u32[]{:S(2)}) collective-permute-start(f32[5,1,128,128]{3,0,2,1:T(8,128)S(1)} %get-tuple-element.10), channel_id=1, source_target_pairs={{32,0},{64,32},{96,64},{128,96},{160,128},{192,160},{224,192},{0,2... | collective-permute-start | bytes 983048 | tf_op jit(solution)/shard_map/ppermute | solution.py:22
  349.4 7.9 %collective-permute-start.6 = (f32[5,6,1,128]{3,0,2,1:T(8,128)S(1)}, f32[5,6,1,128]{3,0,2,1:T(8,128)S(1)}, u32[]{:S(2)}, u32[]{:S(2)}) collective-permute-start(f32[5,6,1,128]{3,0,2,1:T(8,128)S(1)} %get-tuple-element.5), channel_id=1, source_target_pairs={{0,1},{1,2},{2,3},{3,4},{4,5},{5,6},{6,7},{7,8},{8,9},{9,10},{10,1... | collective-permute-start | bytes 46088 | tf_op jit(solution)/shard_map/ppermute | solution.py:19
  349.4 7.8 %collective-permute-start.7 = (f32[5,6,1,128]{3,0,2,1:T(8,128)S(1)}, f32[5,6,1,128]{3,0,2,1:T(8,128)S(1)}, u32[]{:S(2)}, u32[]{:S(2)}) collective-permute-start(f32[5,6,1,128]{3,0,2,1:T(8,128)S(1)} %get-tuple-element.6), channel_id=1, source_target_pairs={{1,0},{2,1},{3,2},{4,3},{5,4},{6,5},{7,6},{8,7},{9,8},{10,9},{11,1... | collective-permute-start | bytes 46088 | tf_op jit(solution)/shard_map/ppermute | solution.py:22
Sparse Core Ops, SparseCore 0:
  49.5 269.4 all-reduce.4
